TPU v7x, 256 devices: a whole 4x4x8 slice. The times are simulated.
256 devices in a mesh: grid: 16 (over y_hi, z), states: 16 (over y_lo, x, core).
Axes of the slice: x: 4, y: 4 (y_hi: 2, y_lo: 2; y = y_hi * 2 + y_lo), z: 8, core: 2. Of those that a mesh axis runs over, the one named last changes fastest.
Arguments:
- states_in: float32 [16, 256, 32, 128], P('states', 'grid'), may hold values from -10 to 10
- potential: float32 [256, 32, 128], P('grid'), may hold values from -2 to 0.5
- projectors: bfloat16 [16, 32, 8, 4096], P('grid', 'states'), may hold values from -0.0625 to 0.0625
- proj_gains: bfloat16 [16, 32, 8], P('grid', 'states'), may hold values from 1 to 6
- atom_owner: int32 [160], P('grid'), may hold values from 0 to 15, as said below
- atom_rows: int32 [160, 32], P('grid'), may hold values from -1 to 8191, as said below
- wrap_rows: int32 [32], replicated, may hold values from 0 to 31, as said below
Outputs:
- filtered: float32 [16, 256, 32, 128], P('states', 'grid')
Inputs may be any that keep to these rules, and one draw needn't show every extreme that they name: `atom_owner`: atom a belongs to tile a // 10. At most 2 atoms of one tile share an owner, and one owner takes exactly 2 atoms of every tile. `atom_rows`: A row r is the line of cells at x = r // 32, y = r % 32. Each list holds distinct rows whose x lies in the atom's own tile of 16 planes, followed by -1 entries; each list has 16 rows or more, and the first atom of every tile fills all 32. wrap_rows[y] = (y + t) mod 32 for one t of 1 to 31.
All inputs are finite; a program needn't handle non-finite values.
Results may differ from a plain program's by a relative error of at most 0.00082.
Values may be sent and summed in bfloat16 or wider, within the bound.
No kernel may reach another device: no remote copies, remote signals or barrier semaphores. Data moves between devices by JAX's collectives and lax.ppermute only.
A program may use at most 64 MiB of HBM per device.

v0:
```python
import math
import jax
import jax.numpy as jnp
from jax import lax
from jax.sharding import PartitionSpec as P

RADIUS = 6
PAIR_CAP = 2
MIXED_WEIGHT = 0.7
CENTER = 12.0
HALF_WIDTH = 8.0


def padded_2(shard, sides, width):
    for axis, dim in sides:
        count, length = (lax.axis_size(axis), shard.shape[dim])
        up = [(i, (i + 1) % count) for i in range(count)]
        down = [(j, i) for i, j in up]
        last = lax.slice_in_dim(shard, length - width, length, axis=dim)
        initial = lax.slice_in_dim(shard, 0, width, axis=dim)
        before = lax.ppermute(last, axis, up)
        after = lax.ppermute(initial, axis, down)
        shard = jnp.concatenate([before, shard, after], axis=dim)
    return shard


def second_table(radius):
    weights = [-2.0 * sum((1.0 / (k * k) for k in range(1, radius + 1)))]
    for k in range(1, radius + 1):
        weights.append(
            2.0
            * (-1) ** (k + 1)
            * math.factorial(radius) ** 2
            / (k * k * math.factorial(radius - k) * math.factorial(radius + k))
        )
    return weights


def first_table(radius):
    weights = [0.0]
    for k in range(1, radius + 1):
        weights.append(
            (-1) ** (k + 1)
            * math.factorial(radius) ** 2
            / (k * math.factorial(radius - k) * math.factorial(radius + k))
        )
    return weights


def laplacian(padded, plane_count):
    second_weights = second_table(RADIUS)
    first_weights = first_table(RADIUS)
    interior = padded[:, RADIUS : RADIUS + plane_count]
    line_depth = interior.shape[3]
    z_padded = jnp.pad(interior, ((0, 0), (0, 0), (0, 0), (RADIUS, RADIUS)))
    summed = 3.0 * second_weights[0] * interior
    y_slope = jnp.zeros_like(padded)
    for k in range(1, RADIUS + 1):
        summed = summed + second_weights[k] * (
            padded[:, RADIUS + k : RADIUS + k + plane_count]
            + padded[:, RADIUS - k : RADIUS - k + plane_count]
        )
        summed = summed + second_weights[k] * (jnp.roll(interior, -k, 2) + jnp.roll(interior, k, 2))
        summed = summed + second_weights[k] * (
            z_padded[:, :, :, RADIUS + k : RADIUS + k + line_depth]
            + z_padded[:, :, :, RADIUS - k : RADIUS - k + line_depth]
        )
        y_slope = y_slope + first_weights[k] * (jnp.roll(padded, -k, 2) - jnp.roll(padded, k, 2))
    cross_term = jnp.zeros_like(interior)
    for k in range(1, RADIUS + 1):
        cross_term = cross_term + first_weights[k] * (
            y_slope[:, RADIUS + k : RADIUS + k + plane_count]
            - y_slope[:, RADIUS - k : RADIUS - k + plane_count]
        )
    return summed + MIXED_WEIGHT * cross_term


def shards(states_in, potential, projectors, proj_gains, atom_owner, atom_rows, wrap_rows):
    state_count, tile_width, breadth, line_depth = states_in.shape
    n_grid = lax.axis_size("grid")
    n_states = lax.axis_size("states")
    tile_index = lax.axis_index("grid")
    tile_lines = tile_width * breadth
    block_rows = atom_rows.shape[1]
    line_span = block_rows * line_depth
    proj_count = projectors.shape[2]
    home_count = atom_owner.shape[0]
    slot_pairs = projectors.shape[1]
    row_order = jnp.arange(breadth, dtype=jnp.int32)
    unwrap_rows = jnp.sum(
        row_order[None, :] * (wrap_rows[None, :] == row_order[:, None]).astype(jnp.int32), axis=1
    )
    atom_order = jnp.arange(home_count, dtype=jnp.int32)
    same_owner = (atom_owner[:, None] == atom_owner[None, :]) & (
        atom_order[None, :] < atom_order[:, None]
    )
    owner_rank = jnp.sum(same_owner.astype(jnp.int32), axis=1)
    atom_slot = atom_owner * PAIR_CAP + owner_rank
    local_rows = jnp.where(atom_rows >= 0, atom_rows - tile_index * tile_lines, tile_lines)
    gain_lanes = jnp.zeros((1, slot_pairs, proj_count, 128), jnp.bfloat16)
    gain_lanes = gain_lanes.at[..., 0].set(proj_gains)
    packed = jnp.concatenate([projectors, gain_lanes], axis=3)
    pairs = [(o * n_states + t, t * n_states + o) for o in range(n_grid) for t in range(n_states)]
    packed = lax.ppermute(packed, ("grid", "states"), pairs)
    gathered = lax.all_gather(packed[0], "states", axis=0, tiled=True)
    gathered = gathered.reshape(n_states * slot_pairs, proj_count, line_span + 128)
    atom_pack = jnp.take(gathered, atom_slot, axis=0)
    proj_rows = atom_pack[:, :, :line_span].reshape(home_count * proj_count, line_span)
    atom_gain = atom_pack[:, :, line_span].astype(jnp.float32)
    selector = (
        local_rows.reshape(-1)[:, None] == jnp.arange(tile_lines, dtype=jnp.int32)[None, :]
    ).astype(jnp.bfloat16)
    atom_eye = jnp.eye(home_count, dtype=jnp.float32)

    def extended(grid_field):
        padded = padded_2(grid_field, (("grid", 1),), RADIUS)
        low_rim = padded[:, :RADIUS]
        high_rim = padded[:, RADIUS + tile_width :]
        low_rim = jnp.where(tile_index == 0, jnp.take(low_rim, wrap_rows, axis=2), low_rim)
        high_rim = jnp.where(
            tile_index == n_grid - 1, jnp.take(high_rim, unwrap_rows, axis=2), high_rim
        )
        return jnp.concatenate([low_rim, padded[:, RADIUS : RADIUS + tile_width], high_rim], axis=1)

    def nonlocal_part(grid_field):
        lines_here = grid_field.reshape(tile_lines, line_depth).astype(jnp.bfloat16)
        picked = jnp.dot(selector, lines_here, preferred_element_type=jnp.float32)
        picked = picked.astype(jnp.bfloat16).reshape(home_count, line_span)
        every_pair = lax.dot_general(
            proj_rows, picked, (((1,), (1,)), ((), ())), preferred_element_type=jnp.float32
        ).reshape(home_count, proj_count, home_count)
        coefficients = jnp.sum(every_pair * atom_eye[:, None, :], axis=2)
        scaled = (coefficients * atom_gain).astype(jnp.bfloat16)
        block_scaled = (atom_eye.astype(jnp.bfloat16)[:, :, None] * scaled[None, :, :]).reshape(
            home_count, home_count * proj_count
        )
        projected = jnp.dot(block_scaled, proj_rows, preferred_element_type=jnp.float32)
        projected = projected.astype(jnp.bfloat16).reshape(home_count * block_rows, line_depth)
        summed = lax.dot_general(
            selector, projected, (((0,), (0,)), ((), ())), preferred_element_type=jnp.float32
        )
        return summed.reshape(state_count, tile_width, breadth, line_depth)

    def operate(grid_field):
        padded = extended(grid_field)
        return (
            -0.5 * laplacian(padded, tile_width)
            + potential[None] * grid_field
            + nonlocal_part(grid_field)
        )

    def shifted(grid_field):
        return (operate(grid_field) - CENTER * grid_field) / HALF_WIDTH

    first_term = shifted(states_in)
    second_term = 2.0 * shifted(first_term) - states_in
    return 2.0 * shifted(second_term) - first_term


def solution(mesh):
    in_specs = (
        P("states", "grid", None, None),
        P("grid", None, None),
        P("grid", "states", None, None),
        P("grid", "states", None),
        P("grid"),
        P("grid", None),
        P(),
    )
    out_specs = P("states", "grid", None, None)
    return jax.shard_map(shards, mesh=mesh, in_specs=in_specs, out_specs=out_specs, check_vma=False)
```

profile of v0, /device:TPU:2, one launch (start us, length us, event | category | flops | bytes accessed | tf_op | source)
XLA Modules:
  0.0 135.8 jit_solution(8653599819950323269)
XLA Ops:
  7.3 0.9 fusion.328
  8.3 5.2 %collective-permute-start.2 = (bf16[1,2,8,4224]{3,2,0,1:T(8,128)(2,1)S(1)}, bf16[1,2,8,4224]{3,2,0,1:T(8,128)(2,1)S(1)}, u32[]{:S(2)}, u32[]{:S(2)}) collective-permute-start(bf16[1,2,8,4224]{3,2,0,1:T(8,128)(2,1)S(1)} %fusion.328), channel_id=1, source_target_pairs={{0,0},{1,16},{2,32},{3,48},{4,64},{5,80},{6,96},{7,112},{8,128},{9... | collective-permute-start | bytes 405512 | tf_op jit(solution)/shard_map/ppermute | solution.py:104
  13.4 1.0 fusion.419
  14.4 6.3 %collective-permute-start = (f32[1,6,32,128]{3,2,1,0:T(8,128)S(1)}, f32[1,6,32,128]{3,2,1,0:T(8,128)S(1)}, u32[]{:S(2)}, u32[]{:S(2)}) collective-permute-start(f32[1,6,32,128]{3,2,1,0:T(8,128)S(1)} %get-tuple-element.164), channel_id=1, source_target_pairs={{16,0},{32,16},{48,32},{64,48},{80,64},{96,80},{112,96},{128,112},... | collective-permute-start | bytes 294920 | tf_op jit(solution)/shard_map/ppermute | solution.py:22
  20.7 1.0 convert_element_type.119
  23.9 0.8 fusion.412
  25.4 0.8 fusion.414
  26.8 0.9 fusion.416
  32.9 0.8 fusion.418
  36.0 0.8 fusion.76
  36.8 30.0 %all-gather.3.cloned.1.call-done = bf16[1,32,8,4224]{3,2,0,1:T(8,128)(2,1)} async-done(((bf16[1,2,8,4224]{3,2,0,1:T(8,128)(2,1)}), bf16[1,32,8,4224]{3,2,0,1:T(8,128)(2,1)}) %all-gather.3.cloned.1.call-update) | async-done | bytes 2162704 | tf_op jit(solution)/shard_map/all_gather | solution.py:105
  66.8 2.2 %gather_fusion = bf16[10,8,4224]{2,1,0:T(8,128)(2,1)S(1)} fusion(bf16[32,8,4224]{2,1,0:T(8,128)(2,1)} %bitcast.111, s32[1024]{0:T(1024)S(1)} %pad_clamp_fusion), kind=kCustom, calls=%fused_computation.6 | custom fusion | bytes 1351720 | tf_op jit(solution)/shard_map/jit(_take)/gather | solution.py:107
  69.1 0.9 copy_select_fusion
  70.1 1.3 fusion.48
  72.5 4.3 %broadcast_multiply_fusion = (f32[1,16,32,128]{3,2,1,0:T(8,128)S(1)}, bf16[1,16,32,128]{3,2,1,0:T(8,128)(2,1)S(1)}, f32[1,16,32,128]{3,2,1,0:T(8,128)}) fusion(f32[1,16,32,128]{3,2,1,0:T(8,128)S(1)} %copy-done, bf16[320,128,1]{1,0,2:T(8,128)(2,1)S(1)} %reshape.2362, s32[16,32]{1,0:T(8,128)S(1)} %multiply_add_fusion, s32[320]{0:T(512)} %copy-done.55, ...), kind=kOutput, calls=%fused_computation.493 | convolution fusion | flops 49053696 | bytes 7752960 | tf_op jit(solution)/shard_map/dot_general | solution.py:139
  79.6 0.8 fusion.401
  81.1 0.8 fusion.403
  81.9 0.8 fusion.405
  83.1 1.3 fusion.49
  85.0 5.6 %collective-permute-start.3 = (f32[1,6,32,128]{3,2,1,0:T(8,128)S(1)}, f32[1,6,32,128]{3,2,1,0:T(8,128)S(1)}, u32[]{:S(2)}, u32[]{:S(2)}) collective-permute-start(f32[1,6,32,128]{3,2,1,0:T(8,128)S(1)} %get-tuple-element.136), channel_id=1, source_target_pairs={{16,0},{32,16},{48,32},{64,48},{80,64},{96,80},{112,96},{128,112},... | collective-permute-start | bytes 294920 | tf_op jit(solution)/shard_map/ppermute | solution.py:22
  91.9 1.1 collective-permute-done.3
  93.7 5.2 %collective-permute-done.4 = f32[1,6,32,128]{3,2,1,0:T(8,128)S(1)} collective-permute-done((f32[1,6,32,128]{3,2,1,0:T(8,128)S(1)}, f32[1,6,32,128]{3,2,1,0:T(8,128)S(1)}, u32[]{:S(2)}, u32[]{:S(2)}) %collective-permute-start.4) | collective-permute-done | bytes 98336 | tf_op jit(solution)/shard_map/ppermute | solution.py:21
  102.0 0.8 fusion.67
  103.6 1.4 %fusion.420 = (bf16[1,16,32,128]{3,2,1,0:T(8,128)(2,1)S(1)}, f32[1,16,32,128]{3,2,1,0:T(8,128)S(1)}) fusion(f32[1,16,32,128]{3,2,1,0:T(8,128)S(1)} %copy-done, f32[1,16,32,128]{3,2,1,0:T(8,128)S(1)} %copy-done.63, bf16[320,128,1]{1,0,2:T(8,128)(2,1)S(1)} %copy-done.18, s32[16,32]{1,0:T(8,128)S(1)} %multiply_add_fusion, s32[320]{0:T(512)S(1)} %copy-done.57, ...), kind=kOutput, calls=%fused_computation.611 | convolution fusion | flops 49119232 | bytes 8015104 | tf_op jit(solution)/shard_map/dot_general | solution.py:139
  107.8 0.8 fusion.386
  109.3 0.8 fusion.384
  110.8 0.8 fusion.382
  112.0 1.3 fusion.50
  113.9 5.6 %collective-permute-start.5 = (f32[1,6,32,128]{3,2,1,0:T(8,128)S(1)}, f32[1,6,32,128]{3,2,1,0:T(8,128)S(1)}, u32[]{:S(2)}, u32[]{:S(2)}) collective-permute-start(f32[1,6,32,128]{3,2,1,0:T(8,128)S(1)} %get-tuple-element.110), channel_id=1, source_target_pairs={{16,0},{32,16},{48,32},{64,48},{80,64},{96,80},{112,96},{128,112},... | collective-permute-start | bytes 294920 | tf_op jit(solution)/shard_map/ppermute | solution.py:22
  120.2 1.9 %collective-permute-done.6 = f32[1,6,32,128]{3,2,1,0:T(8,128)S(1)} collective-permute-done((f32[1,6,32,128]{3,2,1,0:T(8,128)S(1)}, f32[1,6,32,128]{3,2,1,0:T(8,128)S(1)}, u32[]{:S(2)}, u32[]{:S(2)}) %collective-permute-start.6) | collective-permute-done | bytes 98336 | tf_op jit(solution)/shard_map/ppermute | solution.py:21
  124.6 0.8 fusion.58
  126.2 2.7 %fusion.27 = f32[1,16,32,128]{3,2,1,0:T(8,128)} fusion(bf16[320,128,1]{1,0,2:T(8,128)(2,1)S(1)} %reshape.2368, s32[16,32]{1,0:T(8,128)S(1)} %multiply_add_fusion, s32[320]{0:T(512)S(1)} %copy-done.58, f32[1,16,32,128]{3,2,1,0:T(8,128)S(1)} %get-tuple-element.168, f32[1,6,32,128]{3,2,1,0:T(8,128)S(1)} %fusion.329, f32[1,6,32,128]{3,2,1,0:T(8,128)S(1)} %fusion.330, ...), kind=kOutput, calls=%fused_computation.61 | convolution fusion | flops 49119232 | bytes 7621888 | tf_op jit(solution)/shard_map/dot_general | solution.py:139
  (254 shorter events, 30.8 us)
Async XLA Ops:
  6.5 15.9 %copy-start = (f32[1,16,32,128]{3,2,1,0:T(8,128)S(1)}, f32[1,16,32,128]{3,2,1,0:T(8,128)}, u32[]{:S(2)}) copy-start(f32[1,16,32,128]{3,2,1,0:T(8,128)} %param.11) | copy-start | bytes 786436
  6.5 15.7 %copy-start.62 = (s32[32]{0:T(128)S(1)}, s32[32]{0:T(128)}, u32[]{:S(2)}) copy-start(s32[32]{0:T(128)} %param.17) | copy-start | bytes 388
  6.5 60.3 %all-gather.3.cloned.1.call-start = ((), (), s32[]{:S(2)}) async-start(), calls=%async_computation | async-start | bytes 2297856 | tf_op jit(solution)/shard_map/all_gather | solution.py:105
  8.3 21.9 %collective-permute-start.2 = (bf16[1,2,8,4224]{3,2,0,1:T(8,128)(2,1)S(1)}, bf16[1,2,8,4224]{3,2,0,1:T(8,128)(2,1)S(1)}, u32[]{:S(2)}, u32[]{:S(2)}) collective-permute-start(bf16[1,2,8,4224]{3,2,0,1:T(8,128)(2,1)S(1)} %fusion.328), channel_id=1, source_target_pairs={{0,0},{1,16},{2,32},{3,48},{4,64},{5,80},{6,96},{7,112},{8,128},{9... | collective-permute-start | bytes 405512 | tf_op jit(solution)/shard_map/ppermute | solution.py:104
  14.4 19.3 %collective-permute-start = (f32[1,6,32,128]{3,2,1,0:T(8,128)S(1)}, f32[1,6,32,128]{3,2,1,0:T(8,128)S(1)}, u32[]{:S(2)}, u32[]{:S(2)}) collective-permute-start(f32[1,6,32,128]{3,2,1,0:T(8,128)S(1)} %get-tuple-element.164), channel_id=1, source_target_pairs={{16,0},{32,16},{48,32},{64,48},{80,64},{96,80},{112,96},{128,112},... | collective-permute-start | bytes 294920 | tf_op jit(solution)/shard_map/ppermute | solution.py:22
  20.7 13.1 %collective-permute-start.1 = (f32[1,6,32,128]{3,2,1,0:T(8,128)S(1)}, f32[1,6,32,128]{3,2,1,0:T(8,128)S(1)}, u32[]{:S(2)}, u32[]{:S(2)}) collective-permute-start(f32[1,6,32,128]{3,2,1,0:T(8,128)S(1)} %get-tuple-element.165), channel_id=1, source_target_pairs={{0,16},{16,32},{32,48},{48,64},{64,80},{80,96},{96,112},{112,128},... | collective-permute-start | bytes 294920 | tf_op jit(solution)/shard_map/ppermute | solution.py:21
  22.4 12.7 %copy-start.48 = (pred[32]{0:T(512)(128)(4,1)}, pred[32]{0:T(512)(128)(4,1)S(1)}, u32[]{:S(2)}) copy-start(pred[32]{0:T(512)(128)(4,1)S(1)} %compare_and_fusion.1) | copy-start | bytes 100
  22.5 12.7 %copy-start.50 = (pred[32]{0:T(512)(128)(4,1)}, pred[32]{0:T(512)(128)(4,1)S(1)}, u32[]{:S(2)}) copy-start(pred[32]{0:T(512)(128)(4,1)S(1)} %compare_and_fusion) | copy-start | bytes 100
  25.4 3.5 %copy-start.59 = (s32[10]{0:T(128)S(1)}, s32[10]{0:T(128)}, u32[]{:S(2)}) copy-start(s32[10]{0:T(128)} %param.15) | copy-start | bytes 124
  25.4 4.3 %copy-start.38 = (s32[10,32]{1,0:T(8,128)S(1)}, s32[10,32]{1,0:T(8,128)}, u32[]{:S(2)}) copy-start(s32[10,32]{1,0:T(8,128)} %param.16) | copy-start | bytes 3844
  29.8 4.0 %copy-start.55 = (s32[320]{0:T(512)}, s32[320]{0:T(512)S(1)}, u32[]{:S(2)}) copy-start(s32[320]{0:T(512)S(1)} %eq.101) | copy-start | bytes 3844
  33.7 1.5 %copy-start.47 = (s32[1024]{0:T(1024)}, s32[1024]{0:T(1024)S(1)}, u32[]{:S(2)}) copy-start(s32[1024]{0:T(1024)S(1)} %pad_clamp_fusion.1) | copy-start | bytes 12292
  70.0 1.5 %copy-start.52 = (bf16[10,10]{1,0:T(8,128)(2,1)S(1)}, bf16[10,10]{1,0:T(8,128)(2,1)}, u32[]{:S(2)}) copy-start(bf16[10,10]{1,0:T(8,128)(2,1)} %copy.43) | copy-start | bytes 604
  81.1 1.7 %copy-start.56 = (s32[320]{0:T(512)S(1)}, s32[320]{0:T(512)}, u32[]{:S(2)}) copy-start(s32[320]{0:T(512)} %copy-done.55) | copy-start | bytes 3844
  83.1 1.5 %copy-start.53 = (bf16[10,10]{1,0:T(8,128)(2,1)S(1)}, bf16[10,10]{1,0:T(8,128)(2,1)}, u32[]{:S(2)}) copy-start(bf16[10,10]{1,0:T(8,128)(2,1)} %copy.43) | copy-start | bytes 604
  85.0 8.0 %collective-permute-start.3 = (f32[1,6,32,128]{3,2,1,0:T(8,128)S(1)}, f32[1,6,32,128]{3,2,1,0:T(8,128)S(1)}, u32[]{:S(2)}, u32[]{:S(2)}) collective-permute-start(f32[1,6,32,128]{3,2,1,0:T(8,128)S(1)} %get-tuple-element.136), channel_id=1, source_target_pairs={{16,0},{32,16},{48,32},{64,48},{80,64},{96,80},{112,96},{128,112},... | collective-permute-start | bytes 294920 | tf_op jit(solution)/shard_map/ppermute | solution.py:22
  90.6 8.3 %collective-permute-start.4 = (f32[1,6,32,128]{3,2,1,0:T(8,128)S(1)}, f32[1,6,32,128]{3,2,1,0:T(8,128)S(1)}, u32[]{:S(2)}, u32[]{:S(2)}) collective-permute-start(f32[1,6,32,128]{3,2,1,0:T(8,128)S(1)} %get-tuple-element.137), channel_id=1, source_target_pairs={{0,16},{16,32},{32,48},{48,64},{64,80},{80,96},{96,112},{112,128},... | collective-permute-start | bytes 294920 | tf_op jit(solution)/shard_map/ppermute | solution.py:21
  101.9 1.4 %copy-start.15 = (f32[1,16,31,128]{3,2,1,0:T(8,128)S(1)}, f32[1,16,31,128]{3,2,1,0:T(8,128)}, u32[]{:S(2)}) copy-start(f32[1,16,31,128]{3,2,1,0:T(8,128)} %get-tuple-element.135) | copy-start | bytes 761860
  101.9 1.4 %copy-start.18 = (bf16[320,128,1]{1,0,2:T(8,128)(2,1)S(1)}, bf16[320,128,1]{1,0,2:T(8,128)(2,1)}, u32[]{:S(2)}) copy-start(bf16[320,128,1]{1,0,2:T(8,128)(2,1)} %reshape.2365) | copy-start | bytes 245764
  101.9 1.4 %copy-start.23 = (f32[1,16,6,128]{3,2,1,0:T(8,128)S(1)}, f32[1,16,6,128]{3,2,1,0:T(8,128)}, u32[]{:S(2)}) copy-start(f32[1,16,6,128]{3,2,1,0:T(8,128)} %get-tuple-element.112) | copy-start | bytes 147460
  101.9 1.4 %copy-start.26 = (f32[1,16,5,128]{3,2,1,0:T(8,128)S(1)}, f32[1,16,5,128]{3,2,1,0:T(8,128)}, u32[]{:S(2)}) copy-start(f32[1,16,5,128]{3,2,1,0:T(8,128)} %get-tuple-element.117) | copy-start | bytes 122884
  102.0 1.5 %copy-start.60 = (f32[16,32,128]{2,1,0:T(8,128)S(1)}, f32[16,32,128]{2,1,0:T(8,128)}, u32[]{:S(2)}) copy-start(f32[16,32,128]{2,1,0:T(8,128)} %param.12) | copy-start | bytes 786436
  102.0 1.6 %copy-start.63 = (f32[1,16,32,128]{3,2,1,0:T(8,128)S(1)}, f32[1,16,32,128]{3,2,1,0:T(8,128)}, u32[]{:S(2)}) copy-start(f32[1,16,32,128]{3,2,1,0:T(8,128)} %get-tuple-element.166) | copy-start | bytes 786436
  110.1 1.9 %copy-start.41 = (f32[10,10]{0,1:T(8,128)S(1)}, f32[10,10]{0,1:T(8,128)}, u32[]{:S(2)}) copy-start(f32[10,10]{0,1:T(8,128)} %fusion.344) | copy-start | bytes 1204
  111.9 1.5 %copy-start.54 = (bf16[10,10]{1,0:T(8,128)(2,1)S(1)}, bf16[10,10]{1,0:T(8,128)(2,1)}, u32[]{:S(2)}) copy-start(bf16[10,10]{1,0:T(8,128)(2,1)} %copy.43) | copy-start | bytes 604
  113.4 10.2 %copy-start.51 = (pred[32]{0:T(512)(128)(4,1)S(1)}, pred[32]{0:T(512)(128)(4,1)}, u32[]{:S(2)}) copy-start(pred[32]{0:T(512)(128)(4,1)} %copy-done.50) | copy-start | bytes 100
  113.8 9.8 %copy-start.49 = (pred[32]{0:T(512)(128)(4,1)S(1)}, pred[32]{0:T(512)(128)(4,1)}, u32[]{:S(2)}) copy-start(pred[32]{0:T(512)(128)(4,1)} %copy-done.48) | copy-start | bytes 100
  113.8 8.3 %collective-permute-start.6 = (f32[1,6,32,128]{3,2,1,0:T(8,128)S(1)}, f32[1,6,32,128]{3,2,1,0:T(8,128)S(1)}, u32[]{:S(2)}, u32[]{:S(2)}) collective-permute-start(f32[1,6,32,128]{3,2,1,0:T(8,128)S(1)} %get-tuple-element.111), channel_id=1, source_target_pairs={{0,16},{16,32},{32,48},{48,64},{64,80},{80,96},{96,112},{112,128},... | collective-permute-start | bytes 294920 | tf_op jit(solution)/shard_map/ppermute | solution.py:21
  113.9 9.0 %collective-permute-start.5 = (f32[1,6,32,128]{3,2,1,0:T(8,128)S(1)}, f32[1,6,32,128]{3,2,1,0:T(8,128)S(1)}, u32[]{:S(2)}, u32[]{:S(2)}) collective-permute-start(f32[1,6,32,128]{3,2,1,0:T(8,128)S(1)} %get-tuple-element.110), channel_id=1, source_target_pairs={{16,0},{32,16},{48,32},{64,48},{80,64},{96,80},{112,96},{128,112},... | collective-permute-start | bytes 294920 | tf_op jit(solution)/shard_map/ppermute | solution.py:22
  124.5 1.4 %copy-start.8 = (f32[1,16,26,128]{3,2,1,0:T(8,128)S(1)}, f32[1,16,26,128]{3,2,1,0:T(8,128)}, u32[]{:S(2)}) copy-start(f32[1,16,26,128]{3,2,1,0:T(8,128)} %get-tuple-element.89) | copy-start | bytes 638980
  124.6 1.5 %copy-start.61 = (f32[16,32,128]{2,1,0:T(8,128)S(1)}, f32[16,32,128]{2,1,0:T(8,128)}, u32[]{:S(2)}) copy-start(f32[16,32,128]{2,1,0:T(8,128)} %param.12) | copy-start | bytes 786436
  124.6 1.6 %copy-start.64 = (f32[1,16,32,128]{3,2,1,0:T(8,128)S(1)}, f32[1,16,32,128]{3,2,1,0:T(8,128)}, u32[]{:S(2)}) copy-start(f32[1,16,32,128]{3,2,1,0:T(8,128)} %get-tuple-element.166) | copy-start | bytes 786436
  (41 other events, 49.6 us)
Sparse Core Ops, SparseCore 0:
  30.9 35.8 all-gather.2
where the time goes:
time: 136 us
  waiting for transfers between devices  38.2 us (28%)
  local copies, waits for them, and re-layouts  36.5 us (27%)
  starting transfers between devices  22.7 us (17%)
  matrix products  14.8 us (11%)
  between operations  14.7 us (11%)
  other arithmetic  8.83 us (6%)
    all_gather x1, waiting for transfers between devices, shards(): gathered = lax.all_gather(packed[0], 'states', axis=0, tiled=True)  30 us
    slice x36, local copies, waits for them, and re-layouts, laplacian(): jnp.roll(interior, k, 2)  21.6 us
    ppermute x3, starting transfers between devices, padded_2(): after = lax.ppermute(initial, axis, down)  17.5 us
    dot_general x3, matrix products, nonlocal_part(): lax.dot_general(selector, projected, (((0,), (0,)), ((), ())), preferred_...  8.52 us
    ppermute x3, waiting for transfers between devices, padded_2(): before = lax.ppermute(last, axis, up)  7.08 us
    ppermute x1, starting transfers between devices, shards(): packed = lax.ppermute(packed, ('grid', 'states'), pairs)  5.15 us
    dot_general x3, matrix products, nonlocal_part(): lax.dot_general(proj_rows, picked, (((1,), (1,)), ((), ())), preferred_el...  4.03 us
    unnamed x131, local copies, waits for them, and re-layouts  3.33 us
  transfers between devices with their start and end apart: 8, of which 4 were waited for; matrix products, arithmetic and copies ran while one was open for 14% of the time, Pallas kernels for 0%

commit v1 on v0

--- a/solution.py
+++ b/solution.py
@@ -102,7 +102,9 @@
     packed = jnp.concatenate([projectors, gain_lanes], axis=3)
     pairs = [(o * n_states + t, t * n_states + o) for o in range(n_grid) for t in range(n_states)]
     packed = lax.ppermute(packed, ("grid", "states"), pairs)
-    gathered = lax.all_gather(packed[0], "states", axis=0, tiled=True)
+    gathered = jnp.concatenate(
+        lax.all_to_all(jnp.stack([packed[0]] * lax.axis_size("states")), "states", 0, 0), axis=0
+    )
     gathered = gathered.reshape(n_states * slot_pairs, proj_count, line_span + 128)
     atom_pack = jnp.take(gathered, atom_slot, axis=0)
     proj_rows = atom_pack[:, :, :line_span].reshape(home_count * proj_count, line_span)

time: 136 us -> 129 us (0.949)
  between operations: 14.7 us -> 1.42 us
  starting transfers between devices: 22.7 us -> 29.4 us
  waiting for transfers between devices: 38.2 us -> 34.3 us
  local copies, waits for them, and re-layouts: 36.5 us -> 40 us
    all_gather x1 -> x0, waiting for transfers between devices: 30 us -> none  [shards(): gathered = lax.all_gather(packed[0], 'states', axis=0, tiled=True)]
    all_to_all x0 -> x1, waiting for transfers between devices: none -> 26.6 us  [shards(): lax.all_to_all(jnp.stack([packed[0]] * lax.axis_size('states')), 'states'...]
    all_to_all x0 -> x1, starting transfers between devices: none -> 6.57 us  [shards(): lax.all_to_all(jnp.stack([packed[0]] * lax.axis_size('states')), 'states'...]
    gather x1, local copies, waits for them, and re-layouts: 2.24 us -> 0.63 us  [shards(): atom_pack = jnp.take(gathered, atom_slot, axis=0)]
    another operation x0 -> x1, local copies, waits for them, and re-layouts: none -> 1.49 us  [shards(): jnp.stack([packed[0]] * lax.axis_size('states'))]
    unnamed x131 -> x149, local copies, waits for them, and re-layouts: 3.33 us -> 4.12 us
  transfers between devices with their start and end apart: 8 -> 8, of which waited for: 4 -> 4; matrix products, arithmetic and copies ran while one was open for 14% -> 17% of each run, Pallas kernels for 0% -> 0%
where the time goes in v1:
time: 129 us; the launch traced here: 128 us
  local copies, waits for them, and re-layouts  40 us (31%)
  waiting for transfers between devices  34.3 us (27%)
  starting transfers between devices  29.4 us (23%)
  matrix products  14.7 us (11%)
  other arithmetic  8.26 us (6%)
  between operations  1.42 us (1%)
    all_to_all x1, waiting for transfers between devices, shards(): lax.all_to_all(jnp.stack([packed[0]] * lax.axis_size('states')), 'states'...  26.6 us
    slice x36, local copies, waits for them, and re-layouts, laplacian(): jnp.roll(interior, k, 2)  22.5 us
    ppermute x3, starting transfers between devices, padded_2(): after = lax.ppermute(initial, axis, down)  17.6 us
    dot_general x3, matrix products, nonlocal_part(): lax.dot_general(selector, projected, (((0,), (0,)), ((), ())), preferred_...  8.45 us
    ppermute x3, waiting for transfers between devices, padded_2(): before = lax.ppermute(last, axis, up)  6.86 us
    all_to_all x1, starting transfers between devices, shards(): lax.all_to_all(jnp.stack([packed[0]] * lax.axis_size('states')), 'states'...  6.57 us
    ppermute x1, starting transfers between devices, shards(): packed = lax.ppermute(packed, ('grid', 'states'), pairs)  5.15 us
    unnamed x149, local copies, waits for them, and re-layouts  4.12 us
  transfers between devices with their start and end apart: 8, of which 4 were waited for; matrix products, arithmetic and copies ran while one was open for 17% of the time, Pallas kernels for 0%

profile of v1, /device:TPU:2, one launch (start us, length us, event | category | flops | bytes accessed | tf_op | source)
XLA Modules:
  0.0 128.1 jit_solution(15352531437705321686)
XLA Ops:
  0.8 0.9 fusion.328
  1.7 5.2 %collective-permute-start.2 = (bf16[1,2,8,4224]{3,2,1,0:T(8,128)(2,1)S(1)}, bf16[1,2,8,4224]{3,2,1,0:T(8,128)(2,1)S(1)}, u32[]{:S(2)}, u32[]{:S(2)}) collective-permute-start(bf16[1,2,8,4224]{3,2,1,0:T(8,128)(2,1)S(1)} %fusion.328), channel_id=1, source_target_pairs={{0,0},{1,16},{2,32},{3,48},{4,64},{5,80},{6,96},{7,112},{8,128},{9... | collective-permute-start | bytes 405512 | tf_op jit(solution)/shard_map/ppermute | solution.py:104
  6.9 1.0 fusion.419
  7.8 6.3 %collective-permute-start = (f32[1,6,32,128]{3,2,1,0:T(8,128)S(1)}, f32[1,6,32,128]{3,2,1,0:T(8,128)S(1)}, u32[]{:S(2)}, u32[]{:S(2)}) collective-permute-start(f32[1,6,32,128]{3,2,1,0:T(8,128)S(1)} %get-tuple-element.164), channel_id=1, source_target_pairs={{16,0},{32,16},{48,32},{64,48},{80,64},{96,80},{112,96},{128,112},... | collective-permute-start | bytes 294920 | tf_op jit(solution)/shard_map/ppermute | solution.py:22
  14.1 1.0 convert_element_type.119
  15.4 0.8 fusion.408
  16.9 0.8 fusion.410
  18.4 0.8 fusion.412
  19.9 0.9 fusion.414
  21.4 0.8 fusion.416
  22.9 0.9 fusion.418
  29.2 1.5 %stack.3 = bf16[16,2,8,4224]{3,2,1,0:T(8,128)(2,1)} broadcast(bf16[2,8,4224]{2,1,0:T(8,128)(2,1)S(1)} %bitcast.112), dimensions={1,2,3} | broadcast | bytes 2297856 | tf_op jit(solution)/shard_map/stack | solution.py:106
  30.7 6.6 %all-to-all-start = ((bf16[16,2,8,4224]{3,2,1,0:T(8,128)(2,1)}), bf16[16,2,8,4224]{3,2,1,0:T(8,128)(2,1)S(1)}, u32[]{:S(2)}, u32[]{:S(2)}) async-start(bf16[16,2,8,4224]{3,2,1,0:T(8,128)(2,1)} %stack.3), calls=%async_computation | async-start | bytes 4325376 | tf_op jit(solution)/shard_map/all_to_all | solution.py:106
  38.6 1.6 %fusion.76 = f32[1,28,32,128]{3,2,1,0:T(8,128)} fusion(f32[1,6,32,128]{3,2,1,0:T(8,128)S(1)} %fusion.334, f32[1,16,32,128]{3,2,1,0:T(8,128)S(1)} %copy-done, f32[1,6,32,128]{3,2,1,0:T(8,128)S(1)} %fusion.333, f32[1,28,31,128]{3,2,1,0:T(8,128)S(1)} %get-tuple-element.85, f32[1,28,31,128]{3,2,1,0:T(8,128)S(1)} %get-tuple-element.84, ...), kind=kLoop, calls=%fused_computation.173 | loop fusion | flops 3784704 | bytes 6393856 | tf_op jit(solution)/shard_map/add | solution.py:68
  40.2 26.6 %all-to-all-done = bf16[16,2,8,4224]{3,2,1,0:T(8,128)(2,1)S(1)} async-done(((bf16[16,2,8,4224]{3,2,1,0:T(8,128)(2,1)}), bf16[16,2,8,4224]{3,2,1,0:T(8,128)(2,1)S(1)}, u32[]{:S(2)}, u32[]{:S(2)}) %all-to-all-start) | async-done | bytes 2162720 | tf_op jit(solution)/shard_map/all_to_all | solution.py:106
  68.3 1.3 %fusion.48 = f32[10,8]{0,1:T(8,128)S(1)} fusion(bf16[10,4096,1]{1,0,2:T(8,128)(2,1)S(1)} %copy-done.19, bf16[10,8,4224]{2,0,1:T(8,128)(2,1)S(1)} %copy_select_fusion, f32[10,10]{0,1:T(8,128)S(1)} %fusion.344), kind=kOutput, calls=%fused_computation.74 | convolution fusion | flops 6555120 | bytes 1188160 | tf_op jit(solution)/shard_map/dot_general | solution.py:131
  70.9 4.3 %broadcast_multiply_fusion = (f32[1,16,32,128]{3,2,1,0:T(8,128)S(1)}, bf16[1,16,32,128]{3,2,1,0:T(8,128)(2,1)S(1)}, f32[1,16,32,128]{3,2,1,0:T(8,128)}) fusion(f32[1,16,32,128]{3,2,1,0:T(8,128)S(1)} %copy-done, bf16[320,128,1]{1,0,2:T(8,128)(2,1)S(1)} %reshape.2366, s32[16,32]{1,0:T(8,128)S(1)} %multiply_add_fusion, s32[320]{0:T(512)S(1)} %copy-done.64, ...), kind=kOutput, calls=%fused_computation.493 | convolution fusion | flops 49053696 | bytes 7752960 | tf_op jit(solution)/shard_map/dot_general | solution.py:141
  78.6 0.8 fusion.401
  80.0 0.8 fusion.403
  81.5 0.8 fusion.405
  82.7 1.3 %fusion.49 = f32[10,8]{0,1:T(8,128)S(1)} fusion(bf16[10,4096,1]{1,0,2:T(8,128)(2,1)S(1)} %reshape.2367, bf16[10,8,4224]{2,0,1:T(8,128)(2,1)S(1)} %copy_select_fusion, f32[10,10]{0,1:T(8,128)S(1)} %copy-done.47), kind=kOutput, calls=%fused_computation.75 | convolution fusion | flops 6555120 | bytes 1188160 | tf_op jit(solution)/shard_map/dot_general | solution.py:131
  84.6 5.6 %collective-permute-start.3 = (f32[1,6,32,128]{3,2,1,0:T(8,128)S(1)}, f32[1,6,32,128]{3,2,1,0:T(8,128)S(1)}, u32[]{:S(2)}, u32[]{:S(2)}) collective-permute-start(f32[1,6,32,128]{3,2,1,0:T(8,128)S(1)} %get-tuple-element.136), channel_id=1, source_target_pairs={{16,0},{32,16},{48,32},{64,48},{80,64},{96,80},{112,96},{128,112},... | collective-permute-start | bytes 294920 | tf_op jit(solution)/shard_map/ppermute | solution.py:22
  91.5 0.9 collective-permute-done.3
  93.1 5.6 %collective-permute-done.4 = f32[1,6,32,128]{3,2,1,0:T(8,128)S(1)} collective-permute-done((f32[1,6,32,128]{3,2,1,0:T(8,128)}, f32[1,6,32,128]{3,2,1,0:T(8,128)S(1)}, u32[]{:S(2)}, u32[]{:S(2)}) %collective-permute-start.4) | collective-permute-done | bytes 98336 | tf_op jit(solution)/shard_map/ppermute | solution.py:21
  103.4 1.4 %fusion.420 = (bf16[1,16,32,128]{3,2,1,0:T(8,128)(2,1)S(1)}, f32[1,16,32,128]{3,2,1,0:T(8,128)S(1)}) fusion(f32[1,16,32,128]{3,2,1,0:T(8,128)S(1)} %copy-done, f32[1,16,32,128]{3,2,1,0:T(8,128)S(1)} %copy-done.72, bf16[320,128,1]{1,0,2:T(8,128)(2,1)S(1)} %copy-done.21, s32[16,32]{1,0:T(8,128)S(1)} %multiply_add_fusion, s32[320]{0:T(512)S(1)} %copy-done.66, ...), kind=kOutput, calls=%fused_computation.611 | convolution fusion | flops 49119232 | bytes 8015104 | tf_op jit(solution)/shard_map/dot_general | solution.py:141
  106.9 0.8 fusion.386
  108.4 0.8 fusion.384
  109.9 0.8 fusion.382
  111.1 1.3 %fusion.50 = f32[10,8]{0,1:T(8,128)S(1)} fusion(bf16[10,4096,1]{1,0,2:T(8,128)(2,1)S(1)} %reshape.2370, bf16[10,8,4224]{2,0,1:T(8,128)(2,1)S(1)} %copy_select_fusion, f32[10,10]{0,1:T(8,128)S(1)} %copy-done.48), kind=kOutput, calls=%fused_computation.76 | convolution fusion | flops 6555120 | bytes 1188160 | tf_op jit(solution)/shard_map/dot_general | solution.py:131
  113.0 5.6 %collective-permute-start.5 = (f32[1,6,32,128]{3,2,1,0:T(8,128)S(1)}, f32[1,6,32,128]{3,2,1,0:T(8,128)S(1)}, u32[]{:S(2)}, u32[]{:S(2)}) collective-permute-start(f32[1,6,32,128]{3,2,1,0:T(8,128)S(1)} %get-tuple-element.110), channel_id=1, source_target_pairs={{16,0},{32,16},{48,32},{64,48},{80,64},{96,80},{112,96},{128,112},... | collective-permute-start | bytes 294920 | tf_op jit(solution)/shard_map/ppermute | solution.py:22
  119.9 1.3 %collective-permute-done.6 = f32[1,6,32,128]{3,2,1,0:T(8,128)S(1)} collective-permute-done((f32[1,6,32,128]{3,2,1,0:T(8,128)S(1)}, f32[1,6,32,128]{3,2,1,0:T(8,128)S(1)}, u32[]{:S(2)}, u32[]{:S(2)}) %collective-permute-start.6) | collective-permute-done | bytes 98336 | tf_op jit(solution)/shard_map/ppermute | solution.py:21
  125.3 2.8 %fusion.27 = f32[1,16,32,128]{3,2,1,0:T(8,128)} fusion(bf16[320,128,1]{1,0,2:T(8,128)(2,1)S(1)} %copy-done.20, s32[16,32]{1,0:T(8,128)S(1)} %multiply_add_fusion, s32[320]{0:T(512)S(1)} %copy-done.67, f32[1,16,32,128]{3,2,1,0:T(8,128)S(1)} %get-tuple-element.168, f32[1,6,32,128]{3,2,1,0:T(8,128)S(1)} %fusion.329, f32[1,6,32,128]{3,2,1,0:T(8,128)S(1)} %fusion.330, ...), kind=kOutput, calls=%fused_computation.61 | convolution fusion | flops 49119232 | bytes 7621888 | tf_op jit(solution)/shard_map/dot_general | solution.py:141
  (272 shorter events, 34.5 us)
Async XLA Ops:
  0.0 15.4 %copy-start = (f32[1,16,32,128]{3,2,1,0:T(8,128)S(1)}, f32[1,16,32,128]{3,2,1,0:T(8,128)}, u32[]{:S(2)}) copy-start(f32[1,16,32,128]{3,2,1,0:T(8,128)} %param.11) | copy-start | bytes 786436
  0.0 15.2 %copy-start.71 = (s32[32]{0:T(128)S(1)}, s32[32]{0:T(128)}, u32[]{:S(2)}) copy-start(s32[32]{0:T(128)} %param.17) | copy-start | bytes 388
  1.7 27.5 %collective-permute-start.2 = (bf16[1,2,8,4224]{3,2,1,0:T(8,128)(2,1)S(1)}, bf16[1,2,8,4224]{3,2,1,0:T(8,128)(2,1)S(1)}, u32[]{:S(2)}, u32[]{:S(2)}) collective-permute-start(bf16[1,2,8,4224]{3,2,1,0:T(8,128)(2,1)S(1)} %fusion.328), channel_id=1, source_target_pairs={{0,0},{1,16},{2,32},{3,48},{4,64},{5,80},{6,96},{7,112},{8,128},{9... | collective-permute-start | bytes 405512 | tf_op jit(solution)/shard_map/ppermute | solution.py:104
  7.8 19.1 %collective-permute-start = (f32[1,6,32,128]{3,2,1,0:T(8,128)S(1)}, f32[1,6,32,128]{3,2,1,0:T(8,128)S(1)}, u32[]{:S(2)}, u32[]{:S(2)}) collective-permute-start(f32[1,6,32,128]{3,2,1,0:T(8,128)S(1)} %get-tuple-element.164), channel_id=1, source_target_pairs={{16,0},{32,16},{48,32},{64,48},{80,64},{96,80},{112,96},{128,112},... | collective-permute-start | bytes 294920 | tf_op jit(solution)/shard_map/ppermute | solution.py:22
  14.1 12.9 %collective-permute-start.1 = (f32[1,6,32,128]{3,2,1,0:T(8,128)S(1)}, f32[1,6,32,128]{3,2,1,0:T(8,128)S(1)}, u32[]{:S(2)}, u32[]{:S(2)}) collective-permute-start(f32[1,6,32,128]{3,2,1,0:T(8,128)S(1)} %get-tuple-element.165), channel_id=1, source_target_pairs={{0,16},{16,32},{32,48},{48,64},{64,80},{80,96},{96,112},{112,128},... | collective-permute-start | bytes 294920 | tf_op jit(solution)/shard_map/ppermute | solution.py:21
  15.1 52.6 %copy-start.46 = (f32[10,10]{0,1:T(8,128)}, f32[10,10]{0,1:T(8,128)S(1)}, u32[]{:S(2)}) copy-start(f32[10,10]{0,1:T(8,128)S(1)} %fusion.344) | copy-start | bytes 1204
  15.3 13.0 %copy-start.55 = (pred[32]{0:T(512)(128)(4,1)}, pred[32]{0:T(512)(128)(4,1)S(1)}, u32[]{:S(2)}) copy-start(pred[32]{0:T(512)(128)(4,1)S(1)} %compare_and_fusion.1) | copy-start | bytes 100
  15.4 13.0 %copy-start.57 = (pred[32]{0:T(512)(128)(4,1)}, pred[32]{0:T(512)(128)(4,1)S(1)}, u32[]{:S(2)}) copy-start(pred[32]{0:T(512)(128)(4,1)S(1)} %compare_and_fusion) | copy-start | bytes 100
  21.4 3.0 %copy-start.68 = (s32[10]{0:T(128)S(1)}, s32[10]{0:T(128)}, u32[]{:S(2)}) copy-start(s32[10]{0:T(128)} %param.15) | copy-start | bytes 124
  21.4 3.7 %copy-start.45 = (s32[10,32]{1,0:T(8,128)S(1)}, s32[10,32]{1,0:T(8,128)}, u32[]{:S(2)}) copy-start(s32[10,32]{1,0:T(8,128)} %param.16) | copy-start | bytes 3844
  25.2 1.7 %copy-start.63 = (s32[320]{0:T(512)}, s32[320]{0:T(512)S(1)}, u32[]{:S(2)}) copy-start(s32[320]{0:T(512)S(1)} %eq.101) | copy-start | bytes 3844
  26.9 1.6 %copy-start.54 = (s32[1024]{0:T(1024)}, s32[1024]{0:T(1024)S(1)}, u32[]{:S(2)}) copy-start(s32[1024]{0:T(1024)S(1)} %pad_clamp_fusion.1) | copy-start | bytes 12292
  30.7 36.0 %all-to-all-start = ((bf16[16,2,8,4224]{3,2,1,0:T(8,128)(2,1)}), bf16[16,2,8,4224]{3,2,1,0:T(8,128)(2,1)S(1)}, u32[]{:S(2)}, u32[]{:S(2)}) async-start(bf16[16,2,8,4224]{3,2,1,0:T(8,128)(2,1)} %stack.3), calls=%async_computation | async-start | bytes 4325376 | tf_op jit(solution)/shard_map/all_to_all | solution.py:106
  40.2 27.2 %copy-start.62 = (pred[10]{0:T(512)(128)(4,1)S(1)}, pred[10]{0:T(512)(128)(4,1)}, u32[]{:S(2)}) copy-start(pred[10]{0:T(512)(128)(4,1)} %get-tuple-element.18) | copy-start | bytes 34
  67.6 2.1 %copy-start.59 = (bf16[10,10]{1,0:T(8,128)(2,1)S(1)}, bf16[10,10]{1,0:T(8,128)(2,1)}, u32[]{:S(2)}) copy-start(bf16[10,10]{1,0:T(8,128)(2,1)} %copy.51) | copy-start | bytes 604
  80.0 2.3 %copy-start.65 = (s32[320]{0:T(512)S(1)}, s32[320]{0:T(512)}, u32[]{:S(2)}) copy-start(s32[320]{0:T(512)} %copy-done.63) | copy-start | bytes 3844
  80.9 1.8 %copy-start.47 = (f32[10,10]{0,1:T(8,128)S(1)}, f32[10,10]{0,1:T(8,128)}, u32[]{:S(2)}) copy-start(f32[10,10]{0,1:T(8,128)} %copy-done.46) | copy-start | bytes 1204
  82.7 1.4 %copy-start.60 = (bf16[10,10]{1,0:T(8,128)(2,1)S(1)}, bf16[10,10]{1,0:T(8,128)(2,1)}, u32[]{:S(2)}) copy-start(bf16[10,10]{1,0:T(8,128)(2,1)} %copy.51) | copy-start | bytes 604
  84.6 7.9 %collective-permute-start.3 = (f32[1,6,32,128]{3,2,1,0:T(8,128)S(1)}, f32[1,6,32,128]{3,2,1,0:T(8,128)S(1)}, u32[]{:S(2)}, u32[]{:S(2)}) collective-permute-start(f32[1,6,32,128]{3,2,1,0:T(8,128)S(1)} %get-tuple-element.136), channel_id=1, source_target_pairs={{16,0},{32,16},{48,32},{64,48},{80,64},{96,80},{112,96},{128,112},... | collective-permute-start | bytes 294920 | tf_op jit(solution)/shard_map/ppermute | solution.py:22
  90.2 8.4 %collective-permute-start.4 = (f32[1,6,32,128]{3,2,1,0:T(8,128)}, f32[1,6,32,128]{3,2,1,0:T(8,128)S(1)}, u32[]{:S(2)}, u32[]{:S(2)}) collective-permute-start(f32[1,6,32,128]{3,2,1,0:T(8,128)} %get-tuple-element.137), channel_id=1, source_target_pairs={{0,16},{16,32},{32,48},{48,64},{64,80},{80,96},{96,112},{112,128},... | collective-permute-start | bytes 294920 | tf_op jit(solution)/shard_map/ppermute | solution.py:21
  101.7 1.4 %copy-start.21 = (bf16[320,128,1]{1,0,2:T(8,128)(2,1)S(1)}, bf16[320,128,1]{1,0,2:T(8,128)(2,1)}, u32[]{:S(2)}) copy-start(bf16[320,128,1]{1,0,2:T(8,128)(2,1)} %reshape.2369) | copy-start | bytes 245764
  101.7 1.4 %copy-start.32 = (f32[1,16,5,128]{3,2,1,0:T(8,128)S(1)}, f32[1,16,5,128]{3,2,1,0:T(8,128)}, u32[]{:S(2)}) copy-start(f32[1,16,5,128]{3,2,1,0:T(8,128)} %get-tuple-element.117) | copy-start | bytes 122884
  101.8 1.5 %copy-start.69 = (f32[16,32,128]{2,1,0:T(8,128)S(1)}, f32[16,32,128]{2,1,0:T(8,128)}, u32[]{:S(2)}) copy-start(f32[16,32,128]{2,1,0:T(8,128)} %param.12) | copy-start | bytes 786436
  101.8 1.6 %copy-start.72 = (f32[1,16,32,128]{3,2,1,0:T(8,128)S(1)}, f32[1,16,32,128]{3,2,1,0:T(8,128)}, u32[]{:S(2)}) copy-start(f32[1,16,32,128]{3,2,1,0:T(8,128)} %get-tuple-element.166) | copy-start | bytes 786436
  109.2 1.9 %copy-start.48 = (f32[10,10]{0,1:T(8,128)S(1)}, f32[10,10]{0,1:T(8,128)}, u32[]{:S(2)}) copy-start(f32[10,10]{0,1:T(8,128)} %copy-done.46) | copy-start | bytes 1204
  111.0 1.4 %copy-start.61 = (bf16[10,10]{1,0:T(8,128)(2,1)S(1)}, bf16[10,10]{1,0:T(8,128)(2,1)}, u32[]{:S(2)}) copy-start(bf16[10,10]{1,0:T(8,128)(2,1)} %copy.51) | copy-start | bytes 604
  112.9 9.8 %copy-start.58 = (pred[32]{0:T(512)(128)(4,1)S(1)}, pred[32]{0:T(512)(128)(4,1)}, u32[]{:S(2)}) copy-start(pred[32]{0:T(512)(128)(4,1)} %copy-done.57) | copy-start | bytes 100
  112.9 9.8 %copy-start.56 = (pred[32]{0:T(512)(128)(4,1)S(1)}, pred[32]{0:T(512)(128)(4,1)}, u32[]{:S(2)}) copy-start(pred[32]{0:T(512)(128)(4,1)} %copy-done.55) | copy-start | bytes 100
  112.9 8.3 %collective-permute-start.6 = (f32[1,6,32,128]{3,2,1,0:T(8,128)S(1)}, f32[1,6,32,128]{3,2,1,0:T(8,128)S(1)}, u32[]{:S(2)}, u32[]{:S(2)}) collective-permute-start(f32[1,6,32,128]{3,2,1,0:T(8,128)S(1)} %get-tuple-element.111), channel_id=1, source_target_pairs={{0,16},{16,32},{32,48},{48,64},{64,80},{80,96},{96,112},{112,128},... | collective-permute-start | bytes 294920 | tf_op jit(solution)/shard_map/ppermute | solution.py:21
  113.0 9.0 %collective-permute-start.5 = (f32[1,6,32,128]{3,2,1,0:T(8,128)S(1)}, f32[1,6,32,128]{3,2,1,0:T(8,128)S(1)}, u32[]{:S(2)}, u32[]{:S(2)}) collective-permute-start(f32[1,6,32,128]{3,2,1,0:T(8,128)S(1)} %get-tuple-element.110), channel_id=1, source_target_pairs={{16,0},{32,16},{48,32},{64,48},{80,64},{96,80},{112,96},{128,112},... | collective-permute-start | bytes 294920 | tf_op jit(solution)/shard_map/ppermute | solution.py:22
  123.7 1.4 %copy-start.70 = (f32[16,32,128]{2,1,0:T(8,128)S(1)}, f32[16,32,128]{2,1,0:T(8,128)}, u32[]{:S(2)}) copy-start(f32[16,32,128]{2,1,0:T(8,128)} %param.12) | copy-start | bytes 786436
  123.8 1.5 %copy-start.73 = (f32[1,16,32,128]{3,2,1,0:T(8,128)S(1)}, f32[1,16,32,128]{3,2,1,0:T(8,128)}, u32[]{:S(2)}) copy-start(f32[1,16,32,128]{3,2,1,0:T(8,128)} %get-tuple-element.166) | copy-start | bytes 786436
  (50 other events, 61.5 us)
